TPU v7x, 512 devices: a whole 4x8x8 slice. The times are simulated.
512 devices in a mesh: tm: 32 (over y, x), rows: 16 (over z, core).
Axes of the slice: x: 4, y: 8, z: 8, core: 2. Of those that a mesh axis runs over, the one named last changes fastest.
Arguments:
- features: bfloat16 [64, 16, 40, 384], P('tm', 'rows'), may hold values from -6 to 6
- gain_one: float32 [384], replicated, may hold values from 0.1 to 1.9
- weight_one: bfloat16 [384, 3, 3, 3, 384], P('rows'), may hold values from -0.0625 to 0.0625
- bias_one: float32 [384], replicated, may hold values from -3 to 3
- gain_two: float32 [384], replicated, may hold values from 0.1 to 1.9
- weight_two: bfloat16 [384, 3, 3, 3, 384], P('rows'), may hold values from -0.0625 to 0.0625
- bias_two: float32 [384], replicated, may hold values from -3 to 3
Outputs:
- block_out: bfloat16 [64, 16, 40, 384], P('tm', 'rows')
All inputs are finite; a program needn't handle non-finite values.
Results may differ from a plain program's by a relative error of at most 0.0049.
Values may be sent and summed in bfloat16 or wider, within the bound.
No kernel may reach another device: no remote copies, remote signals or barrier semaphores. Data moves between devices by JAX's collectives and lax.ppermute only.
A program may use at most 64 MiB of HBM per device.

v0:
```python
import jax
import jax.numpy as jnp
from jax import lax
from jax.sharding import PartitionSpec as P


def passed_along(x, axis, by):
    peers = lax.axis_size(axis)
    pairs = [(i, i + by) for i in range(peers) if 0 <= i + by < peers]
    return lax.ppermute(x, axis, pairs)


def norm_silu(values, norm_gain):
    values = values.astype(jnp.float32)
    mean_square = jnp.mean(values * values, axis=-1, keepdims=True)
    scaled = values * lax.rsqrt(mean_square + 1e-06) * norm_gain
    return jax.nn.silu(scaled).astype(jnp.bfloat16)


def causal_conv(extended, kernel, bias_part):
    frames = extended.shape[0] - 2
    height = extended.shape[1]
    columns = extended.shape[2]
    channels = extended.shape[3]
    part_width = kernel.shape[0]
    folded = 9 * part_width
    padded_width = (folded + 127) // 128 * 128
    padded = jnp.pad(extended, ((0, 0), (1, 1), (1, 1), (0, 0)))
    summed = jnp.zeros((frames, height, columns, part_width), jnp.float32)
    for tap_time in range(3):
        slab = padded[tap_time : tap_time + frames]
        taps = jnp.transpose(kernel[:, tap_time], (1, 2, 0, 3)).reshape(folded, channels)
        taps = jnp.pad(taps, ((0, padded_width - folded), (0, 0)))
        product = lax.dot_general(
            slab.reshape(-1, channels),
            taps,
            (((1,), (1,)), ((), ())),
            preferred_element_type=jnp.float32,
        )
        product = product[:, :folded].reshape(frames, height + 2, columns + 2, 3, 3, part_width)
        for tap_row in range(3):
            for tap_col in range(3):
                summed = (
                    summed
                    + product[
                        :, tap_row : tap_row + height, tap_col : tap_col + columns, tap_row, tap_col
                    ]
                )
    return summed + bias_part


def shards(features, gain_one, weight_one, bias_one, gain_two, weight_two, bias_two):
    part_width = weight_one.shape[0]
    offset = lax.axis_index("rows") * part_width
    bias_first = lax.dynamic_slice_in_dim(bias_one, offset, part_width, 0)
    bias_second = lax.dynamic_slice_in_dim(bias_two, offset, part_width, 0)
    normed_one = norm_silu(features, gain_one)
    prior_one = passed_along(normed_one, "tm", 1)
    extended_one = jnp.concatenate([prior_one, normed_one], 0)
    full_one = lax.all_gather(extended_one, "rows", axis=1, tiled=True)
    conv_one = causal_conv(full_one, weight_one, bias_first).astype(jnp.bfloat16)
    own_rows = lax.all_to_all(conv_one, "rows", split_axis=1, concat_axis=3, tiled=True)
    normed_two = norm_silu(own_rows, gain_two)
    prior_two = passed_along(normed_two, "tm", 1)
    extended_two = jnp.concatenate([prior_two, normed_two], 0)
    full_two = lax.all_gather(extended_two, "rows", axis=1, tiled=True)
    conv_two = causal_conv(full_two, weight_two, bias_second)
    returned = lax.all_to_all(conv_two, "rows", split_axis=1, concat_axis=3, tiled=True)
    return (features.astype(jnp.float32) + returned).astype(jnp.bfloat16)


def solution(mesh):
    in_specs = (
        P("tm", "rows", None, None),
        P(),
        P("rows", None, None, None, None),
        P(),
        P(),
        P("rows", None, None, None, None),
        P(),
    )
    out_specs = P("tm", "rows", None, None)
    return jax.shard_map(shards, mesh=mesh, in_specs=in_specs, out_specs=out_specs, check_vma=False)
```

profile of v0, /device:TPU:1, one launch (start us, length us, event | category | flops | bytes accessed | tf_op | source)
XLA Modules:
  0.0 217.8 jit_solution(14636832090744077345)
XLA Ops:
  6.5 0.9 fusion.25
  7.5 0.9 fusion.32
  8.4 3.9 %collective-permute-start = (bf16[2,1,40,384]{3,2,1,0:T(8,128)(2,1)S(1)}, bf16[2,1,40,384]{3,2,1,0:T(8,128)(2,1)S(1)}, u32[]{:S(2)}, u32[]{:S(2)}) collective-permute-start(bf16[2,1,40,384]{3,2,1,0:T(8,128)(2,1)S(1)} %fusion.32), channel_id=1, source_target_pairs={{0,16},{16,32},{32,48},{48,64},{64,80},{80,96},{96,112},{112,128},... | collective-permute-start | bytes 184328 | tf_op jit(solution)/shard_map/ppermute | solution.py:10
  12.4 1.3 collective-permute-done
  15.2 1.1 fusion.35
  16.3 48.9 %all-gather.3.cloned.1.call-done = bf16[4,16,40,384]{3,2,0,1:T(8,128)(2,1)} async-done(((bf16[4,1,40,384]{3,2,0,1:T(8,128)(2,1)}), bf16[4,16,40,384]{3,2,0,1:T(8,128)(2,1)}) %all-gather.3.cloned.1.call-update) | async-done | bytes 1966096 | tf_op jit(solution)/shard_map/all_gather | solution.py:60
  65.2 4.8 %pad_slice_fusion.5 = (bf16[2,18,42,384]{3,2,0,1:T(8,128)(2,1)S(1)}, bf16[2,18,42,384]{3,2,0,1:T(8,128)(2,1)}, bf16[2,18,42,384]{3,2,0,1:T(8,128)(2,1)S(1)}) fusion(bf16[4,16,40,384]{3,2,0,1:T(8,128)(2,1)} %all-gather.3.cloned.1.call-done), kind=kLoop, calls=%fused_computation.5 | loop fusion | bytes 5449728 | tf_op jit(solution)/shard_map/slice | solution.py:31
  70.2 1.3 reshape.154
  71.5 1.9 fusion.38
  73.4 4.3 %reshape.156 = f32[2,18,42,3,3,24]{2,1,0,5,4,3:T(8,128)} reshape(f32[1512,216]{0,1:T(8,128)S(1)} %fusion.38) | data formatting | bytes 2612736 | tf_op jit(solution)/shard_map/reshape | solution.py:40
  77.7 1.5 copy.58
  79.2 1.4 reshape.151
  80.5 1.9 fusion.37
  82.4 4.4 %reshape.153 = f32[2,18,42,3,3,24]{2,1,0,5,4,3:T(8,128)} reshape(f32[1512,216]{0,1:T(8,128)S(1)} %fusion.37) | data formatting | bytes 2612736 | tf_op jit(solution)/shard_map/reshape | solution.py:40
  87.9 4.3 %reshape.150 = f32[2,18,42,3,3,24]{2,1,0,5,4,3:T(8,128)} reshape(f32[1512,216]{0,1:T(8,128)S(1)} %fusion.36) | data formatting | bytes 2612736 | tf_op jit(solution)/shard_map/reshape | solution.py:40
  92.2 7.0 %fusion.14 = bf16[2,16,40,24]{2,1,0,3:T(8,128)(2,1)S(1)} fusion(f32[2,18,42,3,3,24]{2,1,0,5,4,3:T(8,128)} %reshape.156, f32[2,18,42,3,3,24]{2,1,0,5,4,3:T(8,128)} %reshape.153, f32[2,18,42,3,3,24]{2,1,0,5,4,3:T(8,128)} %reshape.150, f32[24]{0:T(128)S(1)} %dynamic_slice.6), kind=kLoop, calls=%fused_computation.47 | loop fusion | flops 860160 | bytes 3379296 | tf_op jit(solution)/shard_map/convert_element_type | solution.py:61
  99.6 12.0 %all_to_all.27 = bf16[16,2,960]{2,1,0:T(2,128)(2,1)S(1)} all-to-all(bf16[16,2,960]{2,1,0:T(2,128)(2,1)S(1)} %reshape.192), channel_id=1, replica_groups=mesh['tm'=32,'rows'=16] {'rows'}, dimensions={0} | all-to-all | bytes 122880 | tf_op jit(solution)/shard_map/all_to_all | solution.py:62
  112.7 3.3 %collective-permute-start.1 = (bf16[2,1,40,384]{3,2,1,0:T(8,128)(2,1)S(1)}, bf16[2,1,40,384]{3,2,1,0:T(8,128)(2,1)S(1)}, u32[]{:S(2)}, u32[]{:S(2)}) collective-permute-start(bf16[2,1,40,384]{3,2,1,0:T(8,128)(2,1)S(1)} %multiply_convert_fusion), channel_id=1, source_target_pairs={{0,16},{16,32},{32,48},{48,64},{64,80},{80,96},{96,112},{112,128},... | collective-permute-start | bytes 184328 | tf_op jit(solution)/shard_map/ppermute | solution.py:10
  116.0 1.1 collective-permute-done.1
  118.6 41.3 %all-gather.5.cloned.1.call-done = bf16[4,16,40,384]{3,2,0,1:T(8,128)(2,1)} async-done(((bf16[4,1,40,384]{3,2,0,1:T(8,128)(2,1)}), bf16[4,16,40,384]{3,2,0,1:T(8,128)(2,1)}) %all-gather.5.cloned.1.call-update) | async-done | bytes 1966096 | tf_op jit(solution)/shard_map/all_gather | solution.py:66
  159.9 4.8 %pad_slice_fusion.2 = (bf16[2,18,42,384]{3,2,0,1:T(8,128)(2,1)S(1)}, bf16[2,18,42,384]{3,2,0,1:T(8,128)(2,1)}, bf16[2,18,42,384]{3,2,0,1:T(8,128)(2,1)S(1)}) fusion(bf16[4,16,40,384]{3,2,0,1:T(8,128)(2,1)} %all-gather.5.cloned.1.call-done), kind=kLoop, calls=%fused_computation.2 | loop fusion | bytes 5449728 | tf_op jit(solution)/shard_map/slice | solution.py:31
  164.8 1.3 reshape.163
  166.1 1.9 fusion.41
  168.0 4.3 %reshape.165 = f32[2,18,42,3,3,24]{2,1,0,5,4,3:T(8,128)} reshape(f32[1512,216]{0,1:T(8,128)S(1)} %fusion.41) | data formatting | bytes 2612736 | tf_op jit(solution)/shard_map/reshape | solution.py:40
  172.4 1.5 copy.65
  173.8 1.4 reshape.160
  175.2 1.9 fusion.40
  177.1 4.4 %reshape.162 = f32[2,18,42,3,3,24]{2,1,0,5,4,3:T(8,128)} reshape(f32[1512,216]{0,1:T(8,128)S(1)} %fusion.40) | data formatting | bytes 2612736 | tf_op jit(solution)/shard_map/reshape | solution.py:40
  182.5 4.3 %reshape.159 = f32[2,18,42,3,3,24]{2,1,0,5,4,3:T(8,128)} reshape(f32[1512,216]{0,1:T(8,128)S(1)} %fusion.39) | data formatting | bytes 2612736 | tf_op jit(solution)/shard_map/reshape | solution.py:40
  186.8 7.0 %fusion.1 = f32[2,16,40,24]{2,1,0,3:T(8,128)S(1)} fusion(f32[2,18,42,3,3,24]{2,1,0,5,4,3:T(8,128)} %reshape.165, f32[2,18,42,3,3,24]{2,1,0,5,4,3:T(8,128)} %reshape.162, f32[2,18,42,3,3,24]{2,1,0,5,4,3:T(8,128)} %reshape.159, f32[24]{0:T(128)S(1)} %dynamic_slice.7), kind=kLoop, calls=%fused_computation.8 | loop fusion | flops 829440 | bytes 3440736 | tf_op jit(solution)/shard_map/add | solution.py:49
  194.8 13.2 %all_to_all.28 = f32[16,1,1920]{2,1,0:T(1,128)S(1)} all-to-all(f32[16,1,1920]{2,1,0:T(1,128)S(1)} %reshape.194), channel_id=1, replica_groups=mesh['tm'=32,'rows'=16] {'rows'}, dimensions={0} | all-to-all | bytes 245760 | tf_op jit(solution)/shard_map/all_to_all | solution.py:68
  208.5 0.9 reduce.5
  (38 shorter events, 9.8 us)
Async XLA Ops:
  6.5 58.7 %all-gather.3.cloned.1.call-start = ((), (), s32[]{:S(2)}) async-start(), calls=%async_computation.2 | async-start | bytes 2088960 | tf_op jit(solution)/shard_map/all_gather | solution.py:60
  8.4 5.2 %collective-permute-start = (bf16[2,1,40,384]{3,2,1,0:T(8,128)(2,1)S(1)}, bf16[2,1,40,384]{3,2,1,0:T(8,128)(2,1)S(1)}, u32[]{:S(2)}, u32[]{:S(2)}) collective-permute-start(bf16[2,1,40,384]{3,2,1,0:T(8,128)(2,1)S(1)} %fusion.32), channel_id=1, source_target_pairs={{0,16},{16,32},{32,48},{48,64},{64,80},{80,96},{96,112},{112,128},... | collective-permute-start | bytes 184328 | tf_op jit(solution)/shard_map/ppermute | solution.py:10
  14.3 145.5 %all-gather.5.cloned.1.call-start = ((), (), s32[]{:S(2)}) async-start(), calls=%async_computation.3 | async-start | bytes 2088960 | tf_op jit(solution)/shard_map/all_gather | solution.py:66
  99.2 13.4 %copy-start.2 = (f32[384]{0:T(512)S(1)}, f32[384]{0:T(512)}, u32[]{:S(2)}) copy-start(f32[384]{0:T(512)} %param.11) | copy-start | bytes 4612
  99.3 19.2 %copy-start.1 = (bf16[24,3,3,3,384]{4,0,3,2,1:T(8,128)(2,1)S(1)}, bf16[24,3,3,3,384]{4,0,3,2,1:T(8,128)(2,1)}, u32[]{:S(2)}) copy-start(bf16[24,3,3,3,384]{4,0,3,2,1:T(8,128)(2,1)} %param.12) | copy-start | bytes 1492996
  112.7 4.4 %collective-permute-start.1 = (bf16[2,1,40,384]{3,2,1,0:T(8,128)(2,1)S(1)}, bf16[2,1,40,384]{3,2,1,0:T(8,128)(2,1)S(1)}, u32[]{:S(2)}, u32[]{:S(2)}) collective-permute-start(bf16[2,1,40,384]{3,2,1,0:T(8,128)(2,1)S(1)} %multiply_convert_fusion), channel_id=1, source_target_pairs={{0,16},{16,32},{32,48},{48,64},{64,80},{80,96},{96,112},{112,128},... | collective-permute-start | bytes 184328 | tf_op jit(solution)/shard_map/ppermute | solution.py:10
  193.8 16.5 %copy-start = (bf16[2,1,40,384]{3,2,1,0:T(8,128)(2,1)S(1)}, bf16[2,1,40,384]{3,2,1,0:T(8,128)(2,1)}, u32[]{:S(2)}) copy-start(bf16[2,1,40,384]{3,2,1,0:T(8,128)(2,1)} %param.7) | copy-start | bytes 184324
Sparse Core Ops, SparseCore 0:
  14.5 50.7 all-gather.2
  117.9 41.9 all-gather.4
where the time goes:
time: 218 us
  waiting for transfers between devices  92.6 us (42%)
  local copies, waits for them, and re-layouts  50.8 us (23%)
  blocking collectives  25.2 us (12%)
  other arithmetic  19.4 us (9%)
  between operations  13.6 us (6%)
  matrix products  8.8 us (4%)
  starting transfers between devices  7.28 us (3%)
    all_gather x1, waiting for transfers between devices, shards(): full_one = lax.all_gather(extended_one, 'rows', axis=1, tiled=True)  48.9 us
    all_gather x1, waiting for transfers between devices, shards(): full_two = lax.all_gather(extended_two, 'rows', axis=1, tiled=True)  41.3 us
    reshape x6, local copies, waits for them, and re-layouts, causal_conv(): product[:, :folded]  25.9 us
    all_to_all x1, blocking collectives, shards(): lax.all_to_all(conv_two, 'rows', split_axis=1, concat_axis=3, tiled=True)  13.2 us
    slice x8, local copies, waits for them, and re-layouts, causal_conv(): slab = padded[tap_time:tap_time + frames]  13.1 us
    all_to_all x1, blocking collectives, shards(): lax.all_to_all(conv_one, 'rows', split_axis=1, concat_axis=3, tiled=True)  12 us
    dot_general x6, matrix products, causal_conv(): lax.dot_general(slab.reshape(-1, channels), taps, (((1,), (1,)), ((), ())...  8.8 us
    ppermute x2, starting transfers between devices, passed_along(): return lax.ppermute(x, axis, pairs)  7.24 us
  transfers between devices with their start and end apart: 4, of which 4 were waited for; matrix products, arithmetic and copies ran while one was open for 1% of the time, Pallas kernels for 0%

commit v1 on v0

--- a/solution.py
+++ b/solution.py
@@ -2,6 +2,12 @@
 import jax.numpy as jnp
 from jax import lax
 from jax.sharding import PartitionSpec as P
+
+
+def in_order(blocks, dim):
+    blocks = jnp.moveaxis(blocks, 0, dim)
+    shape = blocks.shape
+    return blocks.reshape(*shape[:dim], shape[dim] * shape[dim + 1], *shape[dim + 2 :])
 
 
 def passed_along(x, axis, by):
@@ -57,7 +63,19 @@
     normed_one = norm_silu(features, gain_one)
     prior_one = passed_along(normed_one, "tm", 1)
     extended_one = jnp.concatenate([prior_one, normed_one], 0)
-    full_one = lax.all_gather(extended_one, "rows", axis=1, tiled=True)
+    size = lax.axis_size("rows")
+    pairs_2 = [(i_2, (i_2 + 1) % size) for i_2 in range(size)]
+    back = [(b, a) for a, b in pairs_2]
+    lower, upper = ([], [])
+    for step in range(size - 1):
+        if step % 2 == 0:
+            lower.append(lax.ppermute(lower[-1] if lower else extended_one, "rows", pairs_2))
+        else:
+            upper.append(lax.ppermute(upper[-1] if upper else extended_one, "rows", back))
+    pieces = jnp.stack([*lower[::-1], extended_one, *upper])
+    shift = lax.axis_index("rows") - len(lower)
+    pieces = pieces[(jnp.arange(size) - shift) % size]
+    full_one = in_order(pieces, 1)
     conv_one = causal_conv(full_one, weight_one, bias_first).astype(jnp.bfloat16)
     own_rows = lax.all_to_all(conv_one, "rows", split_axis=1, concat_axis=3, tiled=True)
     normed_two = norm_silu(own_rows, gain_two)

time: 218 us -> 227 us (1.041)
  starting transfers between devices: 7.28 us -> 45 us
  waiting for transfers between devices: 92.6 us -> 54.9 us
  blocking collectives: 25.2 us -> 31.4 us
  local copies, waits for them, and re-layouts: 50.8 us -> 53.3 us
    all_gather x1 -> x0, waiting for transfers between devices: 48.9 us -> none  [shards(): full_one = lax.all_gather(extended_one, 'rows', axis=1, tiled=True)]
    ppermute x0 -> x15, starting transfers between devices: none -> 36.9 us  [the longest x7 31.2 us: shards(): lax.ppermute(upper[-1] if upper else extended_one, 'rows', back)]
    ppermute x0 -> x15, waiting for transfers between devices: none -> 7.57 us  [the longest x8 6.24 us: shards(): lax.ppermute(lower[-1] if lower else extended_one, 'rows', pairs_2)]
    all_to_all x1, blocking collectives: 12 us -> 18.2 us  [shards(): lax.all_to_all(conv_one, 'rows', split_axis=1, concat_axis=3, tiled=True)]
    all_gather x1, waiting for transfers between devices: 41.3 us -> 45 us  [shards(): full_two = lax.all_gather(extended_two, 'rows', axis=1, tiled=True)]
    gather x0 -> x1, local copies, waits for them, and re-layouts: none -> 2.52 us  [shards(): pieces = pieces[(jnp.arange(size) - shift) % size]]
    slice x8, local copies, waits for them, and re-layouts: 13.1 us -> 10.6 us  [causal_conv(): slab = padded[tap_time:tap_time + frames]]
  transfers between devices with their start and end apart: 4 -> 18, of which waited for: 4 -> 15; matrix products, arithmetic and copies ran while one was open for 1% -> 2% of each run, Pallas kernels for 0% -> 0%
where the time goes in v1:
time: 227 us; the launch traced here: 226 us
  waiting for transfers between devices  54.9 us (24%)
  local copies, waits for them, and re-layouts  53.3 us (23%)
  starting transfers between devices  45 us (20%)
  blocking collectives  31.4 us (14%)
  other arithmetic  18.8 us (8%)
  between operations  13.8 us (6%)
  matrix products  8.78 us (4%)
    all_gather x1, waiting for transfers between devices, shards(): full_two = lax.all_gather(extended_two, 'rows', axis=1, tiled=True)  45 us
    ppermute x7, starting transfers between devices, shards(): lax.ppermute(upper[-1] if upper else extended_one, 'rows', back)  31.2 us
    reshape x6, local copies, waits for them, and re-layouts, causal_conv(): product[:, :folded]  26.1 us
    all_to_all x1, blocking collectives, shards(): lax.all_to_all(conv_one, 'rows', split_axis=1, concat_axis=3, tiled=True)  18.2 us
    all_to_all x1, blocking collectives, shards(): lax.all_to_all(conv_two, 'rows', split_axis=1, concat_axis=3, tiled=True)  13.2 us
    slice x8, local copies, waits for them, and re-layouts, causal_conv(): slab = padded[tap_time:tap_time + frames]  10.6 us
    dot_general x6, matrix products, causal_conv(): lax.dot_general(slab.reshape(-1, channels), taps, (((1,), (1,)), ((), ())...  8.78 us
    ppermute x2, starting transfers between devices, passed_along(): return lax.ppermute(x, axis, pairs)  8.11 us
  transfers between devices with their start and end apart: 18, of which 15 were waited for; matrix products, arithmetic and copies ran while one was open for 2% of the time, Pallas kernels for 0%

profile of v1, /device:TPU:1, one launch (start us, length us, event | category | flops | bytes accessed | tf_op | source)
XLA Modules:
  0.0 226.0 jit_solution(16854416410135140723)
XLA Ops:
  8.4 3.9 %collective-permute-start = (bf16[2,1,40,384]{3,2,1,0:T(8,128)(2,1)S(1)}, bf16[2,1,40,384]{3,2,1,0:T(8,128)(2,1)S(1)}, u32[]{:S(2)}, u32[]{:S(2)}) collective-permute-start(bf16[2,1,40,384]{3,2,1,0:T(8,128)(2,1)S(1)} %fusion.32), channel_id=1, source_target_pairs={{0,16},{16,32},{32,48},{48,64},{64,80},{80,96},{96,112},{112,128},... | collective-permute-start | bytes 184328 | tf_op jit(solution)/shard_map/ppermute | solution.py:16
  13.7 3.5 %collective-permute-start.1 = (bf16[4,1,40,384]{3,2,1,0:T(8,128)(2,1)S(1)}, bf16[4,1,40,384]{3,2,1,0:T(8,128)(2,1)S(1)}, u32[]{:S(2)}, u32[]{:S(2)}) collective-permute-start(bf16[4,1,40,384]{3,2,1,0:T(8,128)(2,1)S(1)} %pad_maximum_fusion), channel_id=1, source_target_pairs={{0,1},{1,2},{2,3},{3,4},{4,5},{5,6},{6,7},{7,8},{8,9},{9,10},{10,1... | collective-permute-start | bytes 368648 | tf_op jit(solution)/shard_map/ppermute | solution.py:72
  17.2 2.1 collective-permute-done.1
  19.3 2.2 collective-permute-start.2
  21.5 3.9 %collective-permute-start.9 = (bf16[4,1,40,384]{3,2,1,0:T(8,128)(2,1)S(1)}, bf16[4,1,40,384]{3,2,1,0:T(8,128)(2,1)S(1)}, u32[]{:S(2)}, u32[]{:S(2)}) collective-permute-start(bf16[4,1,40,384]{3,2,1,0:T(8,128)(2,1)S(1)} %pad_maximum_fusion), channel_id=1, source_target_pairs={{1,0},{2,1},{3,2},{4,3},{5,4},{6,5},{7,6},{8,7},{9,8},{10,9},{11,1... | collective-permute-start | bytes 368648 | tf_op jit(solution)/shard_map/ppermute | solution.py:74
  26.4 4.5 %collective-permute-start.10 = (bf16[4,1,40,384]{3,2,1,0:T(8,128)(2,1)S(1)}, bf16[4,1,40,384]{3,2,1,0:T(8,128)(2,1)S(1)}, u32[]{:S(2)}, u32[]{:S(2)}) collective-permute-start(bf16[4,1,40,384]{3,2,1,0:T(8,128)(2,1)S(1)} %collective-permute-done.9), channel_id=1, source_target_pairs={{1,0},{2,1},{3,2},{4,3},{5,4},{6,5},{7,6},{8,7},{9,8},{10,9},{11,1... | collective-permute-start | bytes 368648 | tf_op jit(solution)/shard_map/ppermute | solution.py:74
  31.9 4.5 %collective-permute-start.11 = (bf16[4,1,40,384]{3,2,1,0:T(8,128)(2,1)S(1)}, bf16[4,1,40,384]{3,2,1,0:T(8,128)(2,1)S(1)}, u32[]{:S(2)}, u32[]{:S(2)}) collective-permute-start(bf16[4,1,40,384]{3,2,1,0:T(8,128)(2,1)S(1)} %collective-permute-done.10), channel_id=1, source_target_pairs={{1,0},{2,1},{3,2},{4,3},{5,4},{6,5},{7,6},{8,7},{9,8},{10,9},{11,1... | collective-permute-start | bytes 368648 | tf_op jit(solution)/shard_map/ppermute | solution.py:74
  37.4 4.5 %collective-permute-start.12 = (bf16[4,1,40,384]{3,2,1,0:T(8,128)(2,1)S(1)}, bf16[4,1,40,384]{3,2,1,0:T(8,128)(2,1)S(1)}, u32[]{:S(2)}, u32[]{:S(2)}) collective-permute-start(bf16[4,1,40,384]{3,2,1,0:T(8,128)(2,1)S(1)} %collective-permute-done.11), channel_id=1, source_target_pairs={{1,0},{2,1},{3,2},{4,3},{5,4},{6,5},{7,6},{8,7},{9,8},{10,9},{11,1... | collective-permute-start | bytes 368648 | tf_op jit(solution)/shard_map/ppermute | solution.py:74
  42.9 4.5 %collective-permute-start.13 = (bf16[4,1,40,384]{3,2,1,0:T(8,128)(2,1)S(1)}, bf16[4,1,40,384]{3,2,1,0:T(8,128)(2,1)S(1)}, u32[]{:S(2)}, u32[]{:S(2)}) collective-permute-start(bf16[4,1,40,384]{3,2,1,0:T(8,128)(2,1)S(1)} %collective-permute-done.12), channel_id=1, source_target_pairs={{1,0},{2,1},{3,2},{4,3},{5,4},{6,5},{7,6},{8,7},{9,8},{10,9},{11,1... | collective-permute-start | bytes 368648 | tf_op jit(solution)/shard_map/ppermute | solution.py:74
  48.3 1.9 fusion.37
  50.2 4.7 %collective-permute-start.14 = (bf16[4,1,40,384]{3,2,1,0:T(8,128)(2,1)S(1)}, bf16[4,1,40,384]{3,2,1,0:T(8,128)(2,1)S(1)}, u32[]{:S(2)}, u32[]{:S(2)}) collective-permute-start(bf16[4,1,40,384]{3,2,1,0:T(8,128)(2,1)S(1)} %collective-permute-done.13), channel_id=1, source_target_pairs={{1,0},{2,1},{3,2},{4,3},{5,4},{6,5},{7,6},{8,7},{9,8},{10,9},{11,1... | collective-permute-start | bytes 368648 | tf_op jit(solution)/shard_map/ppermute | solution.py:74
  55.8 4.4 %collective-permute-start.15 = (bf16[4,1,40,384]{3,2,1,0:T(8,128)(2,1)S(1)}, bf16[4,1,40,384]{3,2,1,0:T(8,128)(2,1)S(1)}, u32[]{:S(2)}, u32[]{:S(2)}) collective-permute-start(bf16[4,1,40,384]{3,2,1,0:T(8,128)(2,1)S(1)} %collective-permute-done.14), channel_id=1, source_target_pairs={{1,0},{2,1},{3,2},{4,3},{5,4},{6,5},{7,6},{8,7},{9,8},{10,9},{11,1... | collective-permute-start | bytes 368648 | tf_op jit(solution)/shard_map/ppermute | solution.py:74
  62.6 2.5 %gather_fusion = bf16[16,4,40,384]{3,2,1,0:T(8,128)(2,1)S(1)} fusion(bf16[16,4,40,384]{3,2,1,0:T(8,128)(2,1)} %bitcast.279, s32[1024]{0:T(1024)S(1)} %pad_clamp_fusion), kind=kCustom, calls=%fused_computation | custom fusion | bytes 3932224 | tf_op jit(solution)/shard_map/gather | solution.py:77
  65.1 2.3 %pad_slice_fusion.5 = (bf16[2,18,42,384]{3,2,0,1:T(8,128)(2,1)S(1)}, bf16[2,18,42,384]{3,2,0,1:T(8,128)(2,1)}, bf16[2,18,42,384]{3,2,0,1:T(8,128)(2,1)S(1)}) fusion(bf16[4,16,40,384]{3,2,0,1:T(8,128)(2,1)S(1)} %bitcast.278), kind=kLoop, calls=%fused_computation.6 | loop fusion | bytes 5449728 | tf_op jit(solution)/shard_map/slice | solution.py:37
  68.9 1.9 fusion.38
  70.8 4.4 %reshape.203 = f32[2,18,42,3,3,24]{2,1,0,5,4,3:T(8,128)} reshape(f32[1512,216]{0,1:T(8,128)S(1)} %fusion.38) | data formatting | bytes 2612736 | tf_op jit(solution)/shard_map/reshape | solution.py:46
  75.1 1.5 copy.109
  78.0 1.9 fusion.39
  79.9 4.3 %reshape.206 = f32[2,18,42,3,3,24]{2,1,0,5,4,3:T(8,128)} reshape(f32[1512,216]{0,1:T(8,128)S(1)} %fusion.39) | data formatting | bytes 2612736 | tf_op jit(solution)/shard_map/reshape | solution.py:46
  85.3 4.3 %reshape.209 = f32[2,18,42,3,3,24]{2,1,0,5,4,3:T(8,128)} reshape(f32[1512,216]{0,1:T(8,128)S(1)} %fusion.40) | data formatting | bytes 2612736 | tf_op jit(solution)/shard_map/reshape | solution.py:46
  89.6 7.0 %fusion.14 = bf16[2,16,40,24]{2,1,0,3:T(8,128)(2,1)S(1)} fusion(f32[2,18,42,3,3,24]{2,1,0,5,4,3:T(8,128)} %reshape.209, f32[2,18,42,3,3,24]{2,1,0,5,4,3:T(8,128)} %reshape.206, f32[2,18,42,3,3,24]{2,1,0,5,4,3:T(8,128)} %reshape.203, f32[24]{0:T(128)S(1)} %dynamic_slice.6), kind=kLoop, calls=%fused_computation.48 | loop fusion | flops 860160 | bytes 3379296 | tf_op jit(solution)/shard_map/convert_element_type | solution.py:79
  97.1 18.2 %all_to_all.27 = bf16[16,2,960]{2,1,0:T(2,128)(2,1)S(1)} all-to-all(bf16[16,2,960]{2,1,0:T(2,128)(2,1)S(1)} %reshape.255), channel_id=1, replica_groups=mesh['tm'=32,'rows'=16] {'rows'}, dimensions={0} | all-to-all | bytes 122880 | tf_op jit(solution)/shard_map/all_to_all | solution.py:80
  116.3 4.2 %collective-permute-start.16 = (bf16[2,1,40,384]{3,2,1,0:T(8,128)(2,1)S(1)}, bf16[2,1,40,384]{3,2,1,0:T(8,128)(2,1)S(1)}, u32[]{:S(2)}, u32[]{:S(2)}) collective-permute-start(bf16[2,1,40,384]{3,2,1,0:T(8,128)(2,1)S(1)} %multiply_convert_fusion), channel_id=1, source_target_pairs={{0,16},{16,32},{32,48},{48,64},{64,80},{80,96},{96,112},{112,128},... | collective-permute-start | bytes 184328 | tf_op jit(solution)/shard_map/ppermute | solution.py:16
  123.1 45.0 %all-gather.2.cloned.1.call-done = bf16[4,16,40,384]{3,2,0,1:T(8,128)(2,1)} async-done(((bf16[4,1,40,384]{3,2,0,1:T(8,128)(2,1)}), bf16[4,16,40,384]{3,2,0,1:T(8,128)(2,1)}) %all-gather.2.cloned.1.call-update) | async-done | bytes 1966096 | tf_op jit(solution)/shard_map/all_gather | solution.py:84
  168.0 4.8 %pad_slice_fusion.2 = (bf16[2,18,42,384]{3,2,0,1:T(8,128)(2,1)S(1)}, bf16[2,18,42,384]{3,2,0,1:T(8,128)(2,1)}, bf16[2,18,42,384]{3,2,0,1:T(8,128)(2,1)S(1)}) fusion(bf16[4,16,40,384]{3,2,0,1:T(8,128)(2,1)} %all-gather.2.cloned.1.call-done), kind=kLoop, calls=%fused_computation.3 | loop fusion | bytes 5449728 | tf_op jit(solution)/shard_map/slice | solution.py:37
  174.3 1.9 fusion.41
  176.2 4.4 %reshape.212 = f32[2,18,42,3,3,24]{2,1,0,5,4,3:T(8,128)} reshape(f32[1512,216]{0,1:T(8,128)S(1)} %fusion.41) | data formatting | bytes 2612736 | tf_op jit(solution)/shard_map/reshape | solution.py:46
  183.4 1.9 fusion.42
  185.3 4.3 %reshape.215 = f32[2,18,42,3,3,24]{2,1,0,5,4,3:T(8,128)} reshape(f32[1512,216]{0,1:T(8,128)S(1)} %fusion.42) | data formatting | bytes 2612736 | tf_op jit(solution)/shard_map/reshape | solution.py:46
  190.7 4.3 %reshape.218 = f32[2,18,42,3,3,24]{2,1,0,5,4,3:T(8,128)} reshape(f32[1512,216]{0,1:T(8,128)S(1)} %fusion.43) | data formatting | bytes 2612736 | tf_op jit(solution)/shard_map/reshape | solution.py:46
  195.1 7.0 %fusion.1 = f32[2,16,40,24]{2,1,0,3:T(8,128)S(1)} fusion(f32[2,18,42,3,3,24]{2,1,0,5,4,3:T(8,128)} %reshape.218, f32[2,18,42,3,3,24]{2,1,0,5,4,3:T(8,128)} %reshape.215, f32[2,18,42,3,3,24]{2,1,0,5,4,3:T(8,128)} %reshape.212, f32[24]{0:T(128)S(1)} %dynamic_slice.7), kind=kLoop, calls=%fused_computation.9 | loop fusion | flops 829440 | bytes 3440736 | tf_op jit(solution)/shard_map/add | solution.py:55
  203.0 13.2 %all_to_all.28 = f32[16,1,1920]{2,1,0:T(1,128)S(1)} all-to-all(f32[16,1,1920]{2,1,0:T(1,128)S(1)} %reshape.257), channel_id=1, replica_groups=mesh['tm'=32,'rows'=16] {'rows'}, dimensions={0} | all-to-all | bytes 245760 | tf_op jit(solution)/shard_map/all_to_all | solution.py:86
  (90 shorter events, 28.2 us)
Async XLA Ops:
  6.5 161.5 %all-gather.2.cloned.1.call-start = ((), (), s32[]{:S(2)}) async-start(), calls=%async_computation.2 | async-start | bytes 2088960 | tf_op jit(solution)/shard_map/all_gather | solution.py:84
  8.4 5.2 %collective-permute-start = (bf16[2,1,40,384]{3,2,1,0:T(8,128)(2,1)S(1)}, bf16[2,1,40,384]{3,2,1,0:T(8,128)(2,1)S(1)}, u32[]{:S(2)}, u32[]{:S(2)}) collective-permute-start(bf16[2,1,40,384]{3,2,1,0:T(8,128)(2,1)S(1)} %fusion.32), channel_id=1, source_target_pairs={{0,16},{16,32},{32,48},{48,64},{64,80},{80,96},{96,112},{112,128},... | collective-permute-start | bytes 184328 | tf_op jit(solution)/shard_map/ppermute | solution.py:16
  13.7 5.6 %collective-permute-start.1 = (bf16[4,1,40,384]{3,2,1,0:T(8,128)(2,1)S(1)}, bf16[4,1,40,384]{3,2,1,0:T(8,128)(2,1)S(1)}, u32[]{:S(2)}, u32[]{:S(2)}) collective-permute-start(bf16[4,1,40,384]{3,2,1,0:T(8,128)(2,1)S(1)} %pad_maximum_fusion), channel_id=1, source_target_pairs={{0,1},{1,2},{2,3},{3,4},{4,5},{5,6},{6,7},{7,8},{8,9},{9,10},{10,1... | collective-permute-start | bytes 368648 | tf_op jit(solution)/shard_map/ppermute | solution.py:72
  19.3 6.9 %collective-permute-start.2 = (bf16[4,1,40,384]{3,2,1,0:T(8,128)(2,1)S(1)}, bf16[4,1,40,384]{3,2,1,0:T(8,128)(2,1)S(1)}, u32[]{:S(2)}, u32[]{:S(2)}) collective-permute-start(bf16[4,1,40,384]{3,2,1,0:T(8,128)(2,1)S(1)} %collective-permute-done.1), channel_id=1, source_target_pairs={{0,1},{1,2},{2,3},{3,4},{4,5},{5,6},{6,7},{7,8},{8,9},{9,10},{10,1... | collective-permute-start | bytes 368648 | tf_op jit(solution)/shard_map/ppermute | solution.py:72
  21.5 4.9 %collective-permute-start.9 = (bf16[4,1,40,384]{3,2,1,0:T(8,128)(2,1)S(1)}, bf16[4,1,40,384]{3,2,1,0:T(8,128)(2,1)S(1)}, u32[]{:S(2)}, u32[]{:S(2)}) collective-permute-start(bf16[4,1,40,384]{3,2,1,0:T(8,128)(2,1)S(1)} %pad_maximum_fusion), channel_id=1, source_target_pairs={{1,0},{2,1},{3,2},{4,3},{5,4},{6,5},{7,6},{8,7},{9,8},{10,9},{11,1... | collective-permute-start | bytes 368648 | tf_op jit(solution)/shard_map/ppermute | solution.py:74
  26.2 5.5 %collective-permute-start.3 = (bf16[4,1,40,384]{3,2,1,0:T(8,128)(2,1)S(1)}, bf16[4,1,40,384]{3,2,1,0:T(8,128)(2,1)S(1)}, u32[]{:S(2)}, u32[]{:S(2)}) collective-permute-start(bf16[4,1,40,384]{3,2,1,0:T(8,128)(2,1)S(1)} %collective-permute-done.2), channel_id=1, source_target_pairs={{0,1},{1,2},{2,3},{3,4},{4,5},{5,6},{6,7},{7,8},{8,9},{9,10},{10,1... | collective-permute-start | bytes 368648 | tf_op jit(solution)/shard_map/ppermute | solution.py:72
  26.4 5.5 %collective-permute-start.10 = (bf16[4,1,40,384]{3,2,1,0:T(8,128)(2,1)S(1)}, bf16[4,1,40,384]{3,2,1,0:T(8,128)(2,1)S(1)}, u32[]{:S(2)}, u32[]{:S(2)}) collective-permute-start(bf16[4,1,40,384]{3,2,1,0:T(8,128)(2,1)S(1)} %collective-permute-done.9), channel_id=1, source_target_pairs={{1,0},{2,1},{3,2},{4,3},{5,4},{6,5},{7,6},{8,7},{9,8},{10,9},{11,1... | collective-permute-start | bytes 368648 | tf_op jit(solution)/shard_map/ppermute | solution.py:74
  31.8 5.5 %collective-permute-start.4 = (bf16[4,1,40,384]{3,2,1,0:T(8,128)(2,1)S(1)}, bf16[4,1,40,384]{3,2,1,0:T(8,128)(2,1)S(1)}, u32[]{:S(2)}, u32[]{:S(2)}) collective-permute-start(bf16[4,1,40,384]{3,2,1,0:T(8,128)(2,1)S(1)} %collective-permute-done.3), channel_id=1, source_target_pairs={{0,1},{1,2},{2,3},{3,4},{4,5},{5,6},{6,7},{7,8},{8,9},{9,10},{10,1... | collective-permute-start | bytes 368648 | tf_op jit(solution)/shard_map/ppermute | solution.py:72
  31.9 5.5 %collective-permute-start.11 = (bf16[4,1,40,384]{3,2,1,0:T(8,128)(2,1)S(1)}, bf16[4,1,40,384]{3,2,1,0:T(8,128)(2,1)S(1)}, u32[]{:S(2)}, u32[]{:S(2)}) collective-permute-start(bf16[4,1,40,384]{3,2,1,0:T(8,128)(2,1)S(1)} %collective-permute-done.10), channel_id=1, source_target_pairs={{1,0},{2,1},{3,2},{4,3},{5,4},{6,5},{7,6},{8,7},{9,8},{10,9},{11,1... | collective-permute-start | bytes 368648 | tf_op jit(solution)/shard_map/ppermute | solution.py:74
  37.3 5.5 %collective-permute-start.5 = (bf16[4,1,40,384]{3,2,1,0:T(8,128)(2,1)S(1)}, bf16[4,1,40,384]{3,2,1,0:T(8,128)(2,1)S(1)}, u32[]{:S(2)}, u32[]{:S(2)}) collective-permute-start(bf16[4,1,40,384]{3,2,1,0:T(8,128)(2,1)S(1)} %collective-permute-done.4), channel_id=1, source_target_pairs={{0,1},{1,2},{2,3},{3,4},{4,5},{5,6},{6,7},{7,8},{8,9},{9,10},{10,1... | collective-permute-start | bytes 368648 | tf_op jit(solution)/shard_map/ppermute | solution.py:72
  37.4 5.5 %collective-permute-start.12 = (bf16[4,1,40,384]{3,2,1,0:T(8,128)(2,1)S(1)}, bf16[4,1,40,384]{3,2,1,0:T(8,128)(2,1)S(1)}, u32[]{:S(2)}, u32[]{:S(2)}) collective-permute-start(bf16[4,1,40,384]{3,2,1,0:T(8,128)(2,1)S(1)} %collective-permute-done.11), channel_id=1, source_target_pairs={{1,0},{2,1},{3,2},{4,3},{5,4},{6,5},{7,6},{8,7},{9,8},{10,9},{11,1... | collective-permute-start | bytes 368648 | tf_op jit(solution)/shard_map/ppermute | solution.py:74
  42.8 5.5 %collective-permute-start.6 = (bf16[4,1,40,384]{3,2,1,0:T(8,128)(2,1)S(1)}, bf16[4,1,40,384]{3,2,1,0:T(8,128)(2,1)S(1)}, u32[]{:S(2)}, u32[]{:S(2)}) collective-permute-start(bf16[4,1,40,384]{3,2,1,0:T(8,128)(2,1)S(1)} %collective-permute-done.5), channel_id=1, source_target_pairs={{0,1},{1,2},{2,3},{3,4},{4,5},{5,6},{6,7},{7,8},{8,9},{9,10},{10,1... | collective-permute-start | bytes 368648 | tf_op jit(solution)/shard_map/ppermute | solution.py:72
  42.9 7.2 %collective-permute-start.13 = (bf16[4,1,40,384]{3,2,1,0:T(8,128)(2,1)S(1)}, bf16[4,1,40,384]{3,2,1,0:T(8,128)(2,1)S(1)}, u32[]{:S(2)}, u32[]{:S(2)}) collective-permute-start(bf16[4,1,40,384]{3,2,1,0:T(8,128)(2,1)S(1)} %collective-permute-done.12), channel_id=1, source_target_pairs={{1,0},{2,1},{3,2},{4,3},{5,4},{6,5},{7,6},{8,7},{9,8},{10,9},{11,1... | collective-permute-start | bytes 368648 | tf_op jit(solution)/shard_map/ppermute | solution.py:74
  48.3 6.6 %collective-permute-start.7 = (bf16[4,1,40,384]{3,2,1,0:T(8,128)(2,1)S(1)}, bf16[4,1,40,384]{3,2,1,0:T(8,128)(2,1)S(1)}, u32[]{:S(2)}, u32[]{:S(2)}) collective-permute-start(bf16[4,1,40,384]{3,2,1,0:T(8,128)(2,1)S(1)} %collective-permute-done.6), channel_id=1, source_target_pairs={{0,1},{1,2},{2,3},{3,4},{4,5},{5,6},{6,7},{7,8},{8,9},{9,10},{10,1... | collective-permute-start | bytes 368648 | tf_op jit(solution)/shard_map/ppermute | solution.py:72
  50.2 5.7 %collective-permute-start.14 = (bf16[4,1,40,384]{3,2,1,0:T(8,128)(2,1)S(1)}, bf16[4,1,40,384]{3,2,1,0:T(8,128)(2,1)S(1)}, u32[]{:S(2)}, u32[]{:S(2)}) collective-permute-start(bf16[4,1,40,384]{3,2,1,0:T(8,128)(2,1)S(1)} %collective-permute-done.13), channel_id=1, source_target_pairs={{1,0},{2,1},{3,2},{4,3},{5,4},{6,5},{7,6},{8,7},{9,8},{10,9},{11,1... | collective-permute-start | bytes 368648 | tf_op jit(solution)/shard_map/ppermute | solution.py:74
  54.9 5.4 %collective-permute-start.8 = (bf16[4,1,40,384]{3,2,1,0:T(8,128)(2,1)S(1)}, bf16[4,1,40,384]{3,2,1,0:T(8,128)(2,1)S(1)}, u32[]{:S(2)}, u32[]{:S(2)}) collective-permute-start(bf16[4,1,40,384]{3,2,1,0:T(8,128)(2,1)S(1)} %collective-permute-done.7), channel_id=1, source_target_pairs={{0,1},{1,2},{2,3},{3,4},{4,5},{5,6},{6,7},{7,8},{8,9},{9,10},{10,1... | collective-permute-start | bytes 368648 | tf_op jit(solution)/shard_map/ppermute | solution.py:72
  55.8 5.4 %collective-permute-start.15 = (bf16[4,1,40,384]{3,2,1,0:T(8,128)(2,1)S(1)}, bf16[4,1,40,384]{3,2,1,0:T(8,128)(2,1)S(1)}, u32[]{:S(2)}, u32[]{:S(2)}) collective-permute-start(bf16[4,1,40,384]{3,2,1,0:T(8,128)(2,1)S(1)} %collective-permute-done.14), channel_id=1, source_target_pairs={{1,0},{2,1},{3,2},{4,3},{5,4},{6,5},{7,6},{8,7},{9,8},{10,9},{11,1... | collective-permute-start | bytes 368648 | tf_op jit(solution)/shard_map/ppermute | solution.py:74
  61.3 1.3 copy-start
  67.4 1.5 copy-start.2
  75.1 2.8 %copy-start.1 = (bf16[24,1,3,3,384]{4,0,3,2,1:T(8,128)(2,1)S(1)}, bf16[24,1,3,3,384]{4,0,3,2,1:T(8,128)(2,1)}, u32[]{:S(2)}) copy-start(bf16[24,1,3,3,384]{4,0,3,2,1:T(8,128)(2,1)} %get-tuple-element.16) | copy-start | bytes 497668
  96.6 19.5 %copy-start.5 = (f32[384]{0:T(512)S(1)}, f32[384]{0:T(512)}, u32[]{:S(2)}) copy-start(f32[384]{0:T(512)} %param.11) | copy-start | bytes 4612
  96.7 26.4 %copy-start.4 = (bf16[24,3,3,3,384]{4,0,3,2,1:T(8,128)(2,1)S(1)}, bf16[24,3,3,3,384]{4,0,3,2,1:T(8,128)(2,1)}, u32[]{:S(2)}) copy-start(bf16[24,3,3,3,384]{4,0,3,2,1:T(8,128)(2,1)} %param.12) | copy-start | bytes 1492996
  116.3 5.3 %collective-permute-start.16 = (bf16[2,1,40,384]{3,2,1,0:T(8,128)(2,1)S(1)}, bf16[2,1,40,384]{3,2,1,0:T(8,128)(2,1)S(1)}, u32[]{:S(2)}, u32[]{:S(2)}) collective-permute-start(bf16[2,1,40,384]{3,2,1,0:T(8,128)(2,1)S(1)} %multiply_convert_fusion), channel_id=1, source_target_pairs={{0,16},{16,32},{32,48},{48,64},{64,80},{80,96},{96,112},{112,128},... | collective-permute-start | bytes 184328 | tf_op jit(solution)/shard_map/ppermute | solution.py:16
  202.1 16.5 %copy-start.3 = (bf16[2,1,40,384]{3,2,1,0:T(8,128)(2,1)S(1)}, bf16[2,1,40,384]{3,2,1,0:T(8,128)(2,1)}, u32[]{:S(2)}) copy-start(bf16[2,1,40,384]{3,2,1,0:T(8,128)(2,1)} %param.7) | copy-start | bytes 184324
Sparse Core Ops, SparseCore 0:
  122.4 45.6 all-gather.1
